TPU v7x, 32 devices: a whole 2x2x4 slice. The times are simulated.
32 devices in a mesh: region: 8 (over y, x, core), dom: 4 (over z).
Axes of the slice: x: 2, y: 2, z: 4, core: 2. Of those that a mesh axis runs over, the one named last changes fastest.
Arguments:
- feats: bfloat16 [16384, 512], P(('region', 'dom')), may hold values from -6 to 6
- hub_feats: bfloat16 [64, 512], P('region'), may hold values from -6 to 6
- hub_ids: int32 [16384, 4], P(('region', 'dom')), may hold values from 0 to 63
- tile_src: int32 [512], P(('region', 'dom')), may hold values from 0 to 4
- tile_mask: int32 [512, 128, 128], P(('region', 'dom')), may hold values 0 or 1
- w_stack: bfloat16 [1024, 512], replicated, may hold values from -0.1875 to 0.1875
- cotangent: bfloat16 [16384, 512], P(('region', 'dom')), may hold values from -6 to 6
Outputs:
- activ: bfloat16 [16384, 512], P(('region', 'dom'))
- weight_grad: float32 [1024, 512], P('dom')
- hub_grad: float32 [64, 512], P('region')
Inputs may be any that keep to these rules, and one draw needn't show every extreme that they name: tile_src names a block of the part's window: 0 is the block taken from the previous part, 1 to 4 are the part's own blocks. `hub_ids`: hub ids index rows of hub_feats.
All inputs are finite; a program needn't handle non-finite values. No bound on the sum of `tile_mask` on one device may be relied on, other than what follows from the above.
Results may differ from a plain program's by a relative error of at most 0.0051.
Values may be sent and summed in bfloat16 or wider, within the bound.
No kernel may reach another device: no remote copies, remote signals or barrier semaphores. Data moves between devices by JAX's collectives and lax.ppermute only.
A program may use at most 64 MiB of HBM per device.

v0:
```python
import jax
import jax.numpy as jnp
from jax import lax
from jax.sharding import PartitionSpec as P


def shifted(value, axis, steps):
    count = lax.axis_size(axis)
    initial, last = (max(0, -steps), min(count, count - steps))
    return lax.ppermute(value, axis, [(source, source + steps) for source in range(initial, last)])


def on_device(feats, hub_feats, hub_ids, tile_src, tile_mask, w_stack, cotangent):
    rows, width = feats.shape
    tile = tile_mask.shape[1]
    nblk = rows // tile
    per_block = tile_src.shape[0] // nblk
    hub_count = hub_ids.shape[1]
    owned = hub_feats.shape[0]
    total_hubs = owned * lax.axis_size("region")
    prev = shifted(feats[rows - tile :], "dom", 1)
    window = jnp.concatenate([prev, feats], axis=0).reshape(nblk + 1, tile, width)
    picked = jnp.take(window, tile_src, axis=0)
    mask_b = tile_mask.astype(jnp.bfloat16)
    prod = jnp.einsum("tij,tjd->tid", mask_b, picked, preferred_element_type=jnp.float32)
    nsum = prod.reshape(nblk, per_block, tile, width).sum(axis=1).reshape(rows, width)
    cnt = tile_mask.reshape(nblk, per_block, tile, tile).sum(axis=(1, 3)).reshape(rows)
    deg = 1.0 + cnt.astype(jnp.float32) + jnp.float32(hub_count)
    hub_cols = lax.broadcasted_iota(jnp.int32, (rows, total_hubs), 1)
    counts = jnp.zeros((rows, total_hubs), jnp.float32)
    for slot in range(hub_count):
        counts = counts + (hub_ids[:, slot : slot + 1] == hub_cols).astype(jnp.float32)
    counts = counts.astype(jnp.bfloat16)
    block = counts
    hsum = jnp.dot(
        block,
        lax.all_gather(hub_feats, "region", axis=0, tiled=True),
        preferred_element_type=jnp.float32,
    )
    agg = ((feats.astype(jnp.float32) + nsum + hsum) / deg[:, None]).astype(jnp.bfloat16)
    inputs = jnp.concatenate([feats, agg], axis=1)
    z = jnp.dot(inputs, w_stack, preferred_element_type=jnp.float32)
    sig = jax.nn.sigmoid(z)
    activ = (z * sig).astype(jnp.bfloat16)
    dz = (cotangent.astype(jnp.float32) * sig * (1.0 + z * (1.0 - sig))).astype(jnp.bfloat16)
    partial_w = lax.psum_scatter(
        lax.dot_general(inputs, dz, (((0,), (0,)), ((), ())), preferred_element_type=jnp.float32),
        "dom",
        scatter_dimension=0,
        tiled=True,
    )
    weight_grad = lax.psum(partial_w, "region")
    dagg = lax.dot_general(
        dz, w_stack[width:], (((1,), (1,)), ((), ())), preferred_element_type=jnp.float32
    )
    sgrad = (dagg / deg[:, None]).astype(jnp.bfloat16)
    block = counts
    region_sum = lax.psum_scatter(
        lax.dot_general(block, sgrad, (((0,), (0,)), ((), ())), preferred_element_type=jnp.float32),
        "region",
        scatter_dimension=0,
        tiled=True,
    )
    hub_grad = lax.psum(region_sum, "dom")
    return (activ, weight_grad, hub_grad)


def solution(mesh):
    placed = (
        P(("region", "dom"), None),
        P("region", None),
        P(("region", "dom"), None),
        P(("region", "dom")),
        P(("region", "dom"), None, None),
        P(),
        P(("region", "dom"), None),
    )
    return jax.shard_map(
        on_device,
        mesh=mesh,
        in_specs=placed,
        out_specs=(P(("region", "dom"), None), P("dom", None), P("region", None)),
        check_vma=False,
    )
```

profile of v0, /device:TPU:0, one launch (start us, length us, event | category | flops | bytes accessed | tf_op | source)
XLA Modules:
  0.0 183.3 jit_solution(3585333480241991576)
XLA Ops:
  7.2 0.0 copy-start
  7.2 0.0 copy-start.2
  7.2 0.0 reduce-scatter.3.cloned.1.call-start
  7.2 1.0 slice.18
  8.2 5.0 %collective-permute-start = (bf16[128,512]{1,0:T(8,128)(2,1)S(1)}, bf16[128,512]{1,0:T(8,128)(2,1)S(1)}, u32[]{:S(2)}, u32[]{:S(2)}) collective-permute-start(bf16[128,512]{1,0:T(8,128)(2,1)S(1)} %slice.18), channel_id=1, source_target_pairs={{0,1},{1,2},{2,3},{4,5},{5,6},{6,7},{8,9},{9,10},{10,11},{12,13},{... | collective-permute-start | bytes 393224 | tf_op jit(solution)/shard_map/ppermute | solution.py:10
  13.2 1.6 reduce_sum.26
  14.8 0.9 fusion.19
  15.6 0.7 compare_select_fusion
  16.3 0.7 compare_and_fusion
  17.0 1.3 copy.23
  18.2 0.0 copy-done.2
  18.2 9.3 %all_gather.3 = bf16[64,512]{1,0:T(8,128)(2,1)S(1)} all-gather(bf16[8,512]{1,0:T(8,128)(2,1)S(1)} %copy-done.2), channel_id=1, replica_groups=mesh['region'=8,'dom'=4] {'region'}, dimensions={0}, use_global_device_ids=true | all-gather | bytes 73728 | tf_op jit(solution)/shard_map/all_gather | solution.py:37
  27.5 0.0 collective-permute-done
  27.5 0.0 copy-done
  27.6 0.0 copy-start.1
  27.6 2.0 %gather_fusion = bf16[16,128,512]{2,1,0:T(8,128)(2,1)} fusion(bf16[5,128,512]{2,1,0:T(8,128)(2,1)S(1)} %bitcast.23, s32[1024]{0:T(1024)S(1)} %pad_clamp_fusion), kind=kCustom, calls=%fused_computation | custom fusion | bytes 4194368 | tf_op jit(solution)/shard_map/jit(_take)/gather | solution.py:23
  29.6 0.0 copy-done.1
  29.6 2.6 %bitcast_reduce_fusion = f32[4,128,512]{1,2,0:T(8,128)S(1)} fusion(bf16[16,128,512]{2,1,0:T(8,128)(2,1)} %gather_fusion, pred[16]{0:T(512)(128)(4,1)S(1)} %compare_and_fusion, s32[16,128,128]{2,1,0:T(8,128)S(1)} %copy-done.1), kind=kOutput, calls=%fused_computation.1 | convolution fusion | flops 270532608 | bytes 4194320 | tf_op jit(solution)/shard_map/tij,tjd->tid/dot_general | solution.py:25
  32.2 0.0 copy-start.3
  32.2 0.0 copy-start.4
  32.2 1.0 fusion.6
  33.2 0.2 copy-done.3
  33.4 0.1 copy-done.4
  33.6 1.9 %multiply_convert_fusion = (bf16[512,512]{1,0:T(8,128)(2,1)S(1)}, bf16[512,512]{1,0:T(8,128)(2,1)}) fusion(bf16[512,512]{1,0:T(8,128)(2,1)S(1)} %copy-done.4, bf16[1024,512]{1,0:T(8,128)(2,1)S(1)} %copy-done.3, bf16[512,512]{0,1:T(8,128)(2,1)S(1)} %fusion.6, bf16[512,512]{0,1:T(8,128)(2,1)S(1)} %copy.23), kind=kOutput, calls=%fused_computation.13 | convolution fusion | flops 542113792 | bytes 3670016 | tf_op jit(solution)/shard_map/dot_general | solution.py:42
  35.5 2.1 %fusion.10 = f32[1024,512]{1,0:T(8,128)} fusion(bf16[512,512]{1,0:T(8,128)(2,1)S(1)} %get-tuple-element.3, bf16[512,512]{0,1:T(8,128)(2,1)S(1)} %fusion.6, bf16[512,512]{0,1:T(8,128)(2,1)S(1)} %copy.23), kind=kOutput, calls=%fused_computation.17 | convolution fusion | flops 538968064 | bytes 3670016 | tf_op jit(solution)/shard_map/dot_general | solution.py:47
  37.5 0.0 reduce-scatter.3.cloned.1.call-update
  37.6 0.0 reduce-scatter.5.cloned.1.call-start
  37.6 1.3 fusion.8
  39.0 0.0 reduce-scatter.5.cloned.1.call-update
  39.0 0.0 all-reduce.2.cloned.1.call-start
  39.0 41.6 %reduce-scatter.3.cloned.1.call-done = f32[256,512]{1,0:T(8,128)} async-done(((f32[1024,512]{1,0:T(8,128)}), f32[256,512]{1,0:T(8,128)}) %reduce-scatter.3.cloned.1.call-update) | async-done | bytes 524304 | tf_op jit(solution)/shard_map/reduce_scatter | solution.py:46
  80.6 0.0 all-reduce.2.cloned.1.call-update
  80.7 36.3 %reduce-scatter.5.cloned.1.call-done = f32[8,512]{1,0:T(8,128)} async-done(((f32[64,512]{1,0:T(8,128)}), f32[8,512]{1,0:T(8,128)}) %reduce-scatter.5.cloned.1.call-update) | async-done | bytes 16400 | tf_op jit(solution)/shard_map/reduce_scatter | solution.py:58
  117.0 19.9 %psum.15 = f32[8,512]{1,0:T(8,128)} all-reduce(f32[8,512]{1,0:T(8,128)} %reduce-scatter.5.cloned.1.call-done), channel_id=1, replica_groups=mesh['region'=8,'dom'=4] {'dom'}, use_global_device_ids=true, to_apply=%region_6.7 | all-reduce | flops 4096 | bytes 32768 | tf_op jit(solution)/shard_map/psum | solution.py:64
  136.9 38.0 %all-reduce.2.cloned.1.call-done = f32[256,512]{1,0:T(8,128)} async-done(((f32[256,512]{1,0:T(8,128)}), f32[256,512]{1,0:T(8,128)}) %all-reduce.2.cloned.1.call-update) | async-done | bytes 524304 | tf_op jit(solution)/shard_map/psum | solution.py:52
  174.9 1.9 %copy.30 = f32[256,512]{1,0:T(8,128)} copy(f32[256,512]{1,0:T(8,128)} %all-reduce.2.cloned.1.call-done) | data formatting | bytes 1048576
  (4 shorter events, 0.1 us)
Async XLA Ops:
  7.2 20.3 %copy-start = (bf16[512,512]{1,0:T(8,128)(2,1)S(1)}, bf16[512,512]{1,0:T(8,128)(2,1)}, u32[]{:S(2)}) copy-start(bf16[512,512]{1,0:T(8,128)(2,1)} %param.7) | copy-start | bytes 1572868
  7.2 11.0 %copy-start.2 = (bf16[8,512]{1,0:T(8,128)(2,1)S(1)}, bf16[8,512]{1,0:T(8,128)(2,1)}, u32[]{:S(2)}) copy-start(bf16[8,512]{1,0:T(8,128)(2,1)} %param.8) | copy-start | bytes 24580
  7.2 73.4 %reduce-scatter.3.cloned.1.call-start = ((), (), s32[]{:S(2)}) async-start(), calls=%async_computation.2 | async-start | bytes 2621440 | tf_op jit(solution)/shard_map/reduce_scatter | solution.py:46
  8.2 19.3 %collective-permute-start = (bf16[128,512]{1,0:T(8,128)(2,1)S(1)}, bf16[128,512]{1,0:T(8,128)(2,1)S(1)}, u32[]{:S(2)}, u32[]{:S(2)}) collective-permute-start(bf16[128,512]{1,0:T(8,128)(2,1)S(1)} %slice.18), channel_id=1, source_target_pairs={{0,1},{1,2},{2,3},{4,5},{5,6},{6,7},{8,9},{9,10},{10,11},{12,13},{... | collective-permute-start | bytes 393224 | tf_op jit(solution)/shard_map/ppermute | solution.py:10
  27.6 2.0 %copy-start.1 = (s32[16,128,128]{2,1,0:T(8,128)S(1)}, s32[16,128,128]{2,1,0:T(8,128)}, u32[]{:S(2)}) copy-start(s32[16,128,128]{2,1,0:T(8,128)} %param.11) | copy-start | bytes 3145732
  32.2 1.2 copy-start.3
  32.2 1.3 copy-start.4
  37.6 79.4 %reduce-scatter.5.cloned.1.call-start = ((), (), s32[]{:S(2)}) async-start(), calls=%async_computation.4 | async-start | bytes 147456 | tf_op jit(solution)/shard_map/reduce_scatter | solution.py:58
  39.0 135.9 %all-reduce.2.cloned.1.call-start = ((), (), s32[]{:S(2)}) async-start(), calls=%async_computation.3 | async-start | bytes 1048576 | tf_op jit(solution)/shard_map/psum | solution.py:52
Sparse Core Ops, SparseCore 0:
  37.7 42.8 reduce-scatter.2
  84.2 32.7 reduce-scatter.4
  120.1 54.7 all-reduce.1
where the time goes:
time: 184 us; the launch traced here: 183 us
  waiting for transfers between devices  116 us (63%)
  blocking collectives  29.2 us (16%)
  between operations  13.9 us (8%)
  matrix products  8.9 us (5%)
  local copies, waits for them, and re-layouts  7.35 us (4%)
  starting transfers between devices  5.08 us (3%)
  other arithmetic  2.97 us (2%)
    reduce_scatter x1, waiting for transfers between devices, on_device(): lax.psum_scatter(lax.dot_general(inputs, dz, (((0,), (0,)), ((), ())), pr...  41.6 us
    psum x1, waiting for transfers between devices, on_device(): weight_grad = lax.psum(partial_w, 'region')  38 us
    reduce_scatter x1, waiting for transfers between devices, on_device(): lax.psum_scatter(lax.dot_general(block, sgrad, (((0,), (0,)), ((), ())),...  36.3 us
    psum x1, blocking collectives, on_device(): hub_grad = lax.psum(region_sum, 'dom')  19.9 us
    all_gather x1, blocking collectives, on_device(): lax.all_gather(hub_feats, 'region', axis=0, tiled=True)  9.26 us
    ppermute x1, starting transfers between devices, shifted(): lax.ppermute(value, axis, [(source, source + steps) for source in range(i...  4.96 us
  transfers between devices with their start and end apart: 4, of which 3 were waited for; matrix products, arithmetic and copies ran while one was open for 3% of the time, Pallas kernels for 0%

commit v1 on v0

--- a/solution.py
+++ b/solution.py
@@ -2,6 +2,24 @@
 import jax.numpy as jnp
 from jax import lax
 from jax.sharding import PartitionSpec as P
+
+
+def gather_around(shard, axis, dim):
+    ways, here, turn = (lax.axis_size(axis), lax.axis_index(axis), shard.shape[dim])
+    shape = [n * ways if d == dim else n for d, n in enumerate(shard.shape)]
+    full = lax.dynamic_update_slice_in_dim(
+        jnp.zeros(shape, shard.dtype), shard, here * turn, axis=dim
+    )
+    going_up = going_down = shard
+    for far in range(1, ways // 2 + 1):
+        going_up = lax.ppermute(going_up, axis, [(d, (d + 1) % ways) for d in range(ways)])
+        full = lax.dynamic_update_slice_in_dim(full, going_up, (here - far) % ways * turn, axis=dim)
+        if 2 * far < ways:
+            going_down = lax.ppermute(going_down, axis, [(d, (d - 1) % ways) for d in range(ways)])
+            full = lax.dynamic_update_slice_in_dim(
+                full, going_down, (here + far) % ways * turn, axis=dim
+            )
+    return full
 
 
 def shifted(value, axis, steps):
@@ -32,11 +50,7 @@
         counts = counts + (hub_ids[:, slot : slot + 1] == hub_cols).astype(jnp.float32)
     counts = counts.astype(jnp.bfloat16)
     block = counts
-    hsum = jnp.dot(
-        block,
-        lax.all_gather(hub_feats, "region", axis=0, tiled=True),
-        preferred_element_type=jnp.float32,
-    )
+    hsum = jnp.dot(block, gather_around(hub_feats, "region", 0), preferred_element_type=jnp.float32)
     agg = ((feats.astype(jnp.float32) + nsum + hsum) / deg[:, None]).astype(jnp.bfloat16)
     inputs = jnp.concatenate([feats, agg], axis=1)
     z = jnp.dot(inputs, w_stack, preferred_element_type=jnp.float32)

time: 184 us -> 190 us (1.033)
  blocking collectives: 29.2 us -> 20 us
  starting transfers between devices: 5.08 us -> 13.1 us
  waiting for transfers between devices: 116 us -> 123 us
    all_gather x1 -> x0, blocking collectives: 9.26 us -> none  [on_device(): lax.all_gather(hub_feats, 'region', axis=0, tiled=True)]
    ppermute x0 -> x7, starting transfers between devices: none -> 8.78 us  [the longest x3 8.17 us: gather_around(): lax.ppermute(going_down, axis, [(d, (d - 1) % ways) for d in range(ways)])]
    ppermute x0 -> x7, waiting for transfers between devices: none -> 6.65 us  [the longest x4 6.58 us: gather_around(): lax.ppermute(going_up, axis, [(d, (d + 1) % ways) for d in range(ways)])]
  transfers between devices with their start and end apart: 4 -> 11, of which waited for: 3 -> 6; matrix products, arithmetic and copies ran while one was open for 3% -> 4% of each run, Pallas kernels for 0% -> 0%
where the time goes in v1:
time: 190 us; the launch traced here: 189 us
  waiting for transfers between devices  123 us (65%)
  blocking collectives  20 us (11%)
  between operations  13.9 us (7%)
  starting transfers between devices  13.1 us (7%)
  matrix products  8.88 us (5%)
  local copies, waits for them, and re-layouts  8 us (4%)
  other arithmetic  2.96 us (2%)
    reduce_scatter x1, waiting for transfers between devices, on_device(): lax.psum_scatter(lax.dot_general(inputs, dz, (((0,), (0,)), ((), ())), pr...  41.6 us
    psum x1, waiting for transfers between devices, on_device(): weight_grad = lax.psum(partial_w, 'region')  38 us
    reduce_scatter x1, waiting for transfers between devices, on_device(): lax.psum_scatter(lax.dot_general(block, sgrad, (((0,), (0,)), ((), ())),...  36.3 us
    psum x1, blocking collectives, on_device(): hub_grad = lax.psum(region_sum, 'dom')  20 us
    ppermute x3, starting transfers between devices, gather_around(): lax.ppermute(going_down, axis, [(d, (d - 1) % ways) for d in range(ways)])  8.17 us
    ppermute x4, waiting for transfers between devices, gather_around(): lax.ppermute(going_up, axis, [(d, (d + 1) % ways) for d in range(ways)])  6.58 us
    ppermute x1, starting transfers between devices, shifted(): lax.ppermute(value, axis, [(source, source + steps) for source in range(i...  4.18 us
  transfers between devices with their start and end apart: 11, of which 6 were waited for; matrix products, arithmetic and copies ran while one was open for 4% of the time, Pallas kernels for 0%

profile of v1, /device:TPU:0, one launch (start us, length us, event | category | flops | bytes accessed | tf_op | source)
XLA Modules:
  0.0 189.5 jit_solution(17576235610270385420)
XLA Ops:
  7.2 0.0 copy-start
  7.2 0.0 reduce-scatter.3.cloned.1.call-start
  7.2 0.5 collective-permute-start.1
  7.8 2.9 %collective-permute-start.2 = (bf16[8,512]{1,0:T(8,128)(2,1)}, bf16[8,512]{1,0:T(8,128)(2,1)S(1)}, u32[]{:S(2)}, u32[]{:S(2)}) collective-permute-start(bf16[8,512]{1,0:T(8,128)(2,1)} %param.8), channel_id=1, source_target_pairs={{0,28},{4,0},{8,4},{12,8},{16,12},{20,16},{24,20},{28,24},{1,29},{... | collective-permute-start | bytes 24584 | tf_op jit(solution)/shard_map/ppermute | solution.py:18
  10.7 0.9 slice.18
  11.6 4.2 %collective-permute-start = (bf16[128,512]{1,0:T(8,128)(2,1)S(1)}, bf16[128,512]{1,0:T(8,128)(2,1)S(1)}, u32[]{:S(2)}, u32[]{:S(2)}) collective-permute-start(bf16[128,512]{1,0:T(8,128)(2,1)S(1)} %slice.18), channel_id=1, source_target_pairs={{0,1},{1,2},{2,3},{4,5},{5,6},{6,7},{8,9},{9,10},{10,11},{12,13},{... | collective-permute-start | bytes 393224 | tf_op jit(solution)/shard_map/ppermute | solution.py:28
  15.8 0.7 compare_select_fusion
  16.5 0.7 compare_and_fusion
  17.1 1.6 reduce_sum.26
  18.7 0.9 fusion.19
  19.6 0.7 constant_dynamic-update-slice_fusion.7
  20.3 1.3 copy.23
  21.6 0.0 collective-permute-done.1
  21.6 0.1 collective-permute-start.3
  21.7 0.0 collective-permute-done.2
  21.7 2.6 %collective-permute-start.4 = (bf16[8,512]{1,0:T(8,128)(2,1)S(1)}, bf16[8,512]{1,0:T(8,128)(2,1)S(1)}, u32[]{:S(2)}, u32[]{:S(2)}) collective-permute-start(bf16[8,512]{1,0:T(8,128)(2,1)S(1)} %collective-permute-done.2), channel_id=1, source_target_pairs={{0,28},{4,0},{8,4},{12,8},{16,12},{20,16},{24,20},{28,24},{1,29},{... | collective-permute-start | bytes 24584 | tf_op jit(solution)/shard_map/ppermute | solution.py:18
  24.3 1.3 collective-permute-done.3
  25.7 0.0 collective-permute-start.5
  25.7 0.0 collective-permute-done.4
  25.7 2.6 %collective-permute-start.6 = (bf16[8,512]{1,0:T(8,128)(2,1)S(1)}, bf16[8,512]{1,0:T(8,128)(2,1)S(1)}, u32[]{:S(2)}, u32[]{:S(2)}) collective-permute-start(bf16[8,512]{1,0:T(8,128)(2,1)S(1)} %collective-permute-done.4), channel_id=1, source_target_pairs={{0,28},{4,0},{8,4},{12,8},{16,12},{20,16},{24,20},{28,24},{1,29},{... | collective-permute-start | bytes 24584 | tf_op jit(solution)/shard_map/ppermute | solution.py:18
  28.3 1.3 collective-permute-done.5
  29.6 0.0 collective-permute-start.7
  29.6 0.0 collective-permute-done.6
  29.7 3.9 %collective-permute-done.7 = bf16[8,512]{1,0:T(8,128)(2,1)S(1)} collective-permute-done((bf16[8,512]{1,0:T(8,128)(2,1)S(1)}, bf16[8,512]{1,0:T(8,128)(2,1)S(1)}, u32[]{:S(2)}, u32[]{:S(2)}) %collective-permute-start.7) | collective-permute-done | bytes 8224 | tf_op jit(solution)/shard_map/ppermute | solution.py:15
  33.6 0.0 collective-permute-done
  33.6 0.0 copy-done
  33.7 0.0 copy-start.1
  33.7 2.0 %gather_fusion = bf16[16,128,512]{2,1,0:T(8,128)(2,1)} fusion(bf16[5,128,512]{2,1,0:T(8,128)(2,1)S(1)} %bitcast.23, s32[1024]{0:T(1024)S(1)} %pad_clamp_fusion), kind=kCustom, calls=%fused_computation | custom fusion | bytes 4194368 | tf_op jit(solution)/shard_map/jit(_take)/gather | solution.py:41
  35.7 0.0 copy-done.1
  35.7 2.6 %bitcast_reduce_fusion = f32[4,128,512]{1,2,0:T(8,128)S(1)} fusion(bf16[16,128,512]{2,1,0:T(8,128)(2,1)} %gather_fusion, pred[16]{0:T(512)(128)(4,1)S(1)} %compare_and_fusion, s32[16,128,128]{2,1,0:T(8,128)S(1)} %copy-done.1), kind=kOutput, calls=%fused_computation.1 | convolution fusion | flops 270532608 | bytes 4194320 | tf_op jit(solution)/shard_map/tij,tjd->tid/dot_general | solution.py:43
  38.3 0.0 copy-start.2
  38.3 0.0 copy-start.3
  38.3 1.0 fusion.6
  39.3 0.2 copy-done.2
  39.5 0.1 copy-done.3
  39.7 1.9 %multiply_convert_fusion = (bf16[512,512]{1,0:T(8,128)(2,1)S(1)}, bf16[512,512]{1,0:T(8,128)(2,1)}) fusion(bf16[512,512]{1,0:T(8,128)(2,1)S(1)} %copy-done.3, bf16[1024,512]{1,0:T(8,128)(2,1)S(1)} %copy-done.2, bf16[512,512]{0,1:T(8,128)(2,1)S(1)} %fusion.6, bf16[512,512]{0,1:T(8,128)(2,1)S(1)} %copy.23), kind=kOutput, calls=%fused_computation.13 | convolution fusion | flops 542113792 | bytes 3670016 | tf_op jit(solution)/shard_map/dot_general | solution.py:56
  41.6 2.0 %fusion.10 = f32[1024,512]{1,0:T(8,128)} fusion(bf16[512,512]{1,0:T(8,128)(2,1)S(1)} %get-tuple-element.3, bf16[512,512]{0,1:T(8,128)(2,1)S(1)} %fusion.6, bf16[512,512]{0,1:T(8,128)(2,1)S(1)} %copy.23), kind=kOutput, calls=%fused_computation.17 | convolution fusion | flops 538968064 | bytes 3670016 | tf_op jit(solution)/shard_map/dot_general | solution.py:61
  43.6 0.0 reduce-scatter.3.cloned.1.call-update
  43.7 0.0 reduce-scatter.5.cloned.1.call-start
  43.7 1.3 fusion.8
  45.0 0.0 reduce-scatter.5.cloned.1.call-update
  45.1 0.0 all-reduce.2.cloned.1.call-start
  45.1 41.6 %reduce-scatter.3.cloned.1.call-done = f32[256,512]{1,0:T(8,128)} async-done(((f32[1024,512]{1,0:T(8,128)}), f32[256,512]{1,0:T(8,128)}) %reduce-scatter.3.cloned.1.call-update) | async-done | bytes 524304 | tf_op jit(solution)/shard_map/reduce_scatter | solution.py:60
  86.8 0.0 all-reduce.2.cloned.1.call-update
  86.8 36.3 %reduce-scatter.5.cloned.1.call-done = f32[8,512]{1,0:T(8,128)} async-done(((f32[64,512]{1,0:T(8,128)}), f32[8,512]{1,0:T(8,128)}) %reduce-scatter.5.cloned.1.call-update) | async-done | bytes 16400 | tf_op jit(solution)/shard_map/reduce_scatter | solution.py:72
  123.1 20.0 %psum.15 = f32[8,512]{1,0:T(8,128)} all-reduce(f32[8,512]{1,0:T(8,128)} %reduce-scatter.5.cloned.1.call-done), channel_id=1, replica_groups=mesh['region'=8,'dom'=4] {'dom'}, use_global_device_ids=true, to_apply=%region_6.7 | all-reduce | flops 4096 | bytes 32768 | tf_op jit(solution)/shard_map/psum | solution.py:78
  143.1 38.0 %all-reduce.2.cloned.1.call-done = f32[256,512]{1,0:T(8,128)} async-done(((f32[256,512]{1,0:T(8,128)}), f32[256,512]{1,0:T(8,128)}) %all-reduce.2.cloned.1.call-update) | async-done | bytes 524304 | tf_op jit(solution)/shard_map/psum | solution.py:66
  181.1 1.9 copy.38
  (12 shorter events, 0.1 us)
Async XLA Ops:
  7.2 26.5 %copy-start = (bf16[512,512]{1,0:T(8,128)(2,1)S(1)}, bf16[512,512]{1,0:T(8,128)(2,1)}, u32[]{:S(2)}) copy-start(bf16[512,512]{1,0:T(8,128)(2,1)} %param.7) | copy-start | bytes 1572868
  7.2 79.6 %reduce-scatter.3.cloned.1.call-start = ((), (), s32[]{:S(2)}) async-start(), calls=%async_computation.2 | async-start | bytes 2621440 | tf_op jit(solution)/shard_map/reduce_scatter | solution.py:60
  7.2 14.4 %collective-permute-start.1 = (bf16[8,512]{1,0:T(8,128)(2,1)}, bf16[8,512]{1,0:T(8,128)(2,1)S(1)}, u32[]{:S(2)}, u32[]{:S(2)}) collective-permute-start(bf16[8,512]{1,0:T(8,128)(2,1)} %param.8), channel_id=1, source_target_pairs={{0,4},{4,8},{8,12},{12,16},{16,20},{20,24},{24,28},{28,0},{1,5},{5... | collective-permute-start | bytes 24584 | tf_op jit(solution)/shard_map/ppermute | solution.py:15
  7.8 13.9 %collective-permute-start.2 = (bf16[8,512]{1,0:T(8,128)(2,1)}, bf16[8,512]{1,0:T(8,128)(2,1)S(1)}, u32[]{:S(2)}, u32[]{:S(2)}) collective-permute-start(bf16[8,512]{1,0:T(8,128)(2,1)} %param.8), channel_id=1, source_target_pairs={{0,28},{4,0},{8,4},{12,8},{16,12},{20,16},{24,20},{28,24},{1,29},{... | collective-permute-start | bytes 24584 | tf_op jit(solution)/shard_map/ppermute | solution.py:18
  11.6 22.0 %collective-permute-start = (bf16[128,512]{1,0:T(8,128)(2,1)S(1)}, bf16[128,512]{1,0:T(8,128)(2,1)S(1)}, u32[]{:S(2)}, u32[]{:S(2)}) collective-permute-start(bf16[128,512]{1,0:T(8,128)(2,1)S(1)} %slice.18), channel_id=1, source_target_pairs={{0,1},{1,2},{2,3},{4,5},{5,6},{6,7},{8,9},{9,10},{10,11},{12,13},{... | collective-permute-start | bytes 393224 | tf_op jit(solution)/shard_map/ppermute | solution.py:28
  21.6 4.0 %collective-permute-start.3 = (bf16[8,512]{1,0:T(8,128)(2,1)S(1)}, bf16[8,512]{1,0:T(8,128)(2,1)S(1)}, u32[]{:S(2)}, u32[]{:S(2)}) collective-permute-start(bf16[8,512]{1,0:T(8,128)(2,1)S(1)} %collective-permute-done.1), channel_id=1, source_target_pairs={{0,4},{4,8},{8,12},{12,16},{16,20},{20,24},{24,28},{28,0},{1,5},{5... | collective-permute-start | bytes 24584 | tf_op jit(solution)/shard_map/ppermute | solution.py:15
  21.7 4.0 %collective-permute-start.4 = (bf16[8,512]{1,0:T(8,128)(2,1)S(1)}, bf16[8,512]{1,0:T(8,128)(2,1)S(1)}, u32[]{:S(2)}, u32[]{:S(2)}) collective-permute-start(bf16[8,512]{1,0:T(8,128)(2,1)S(1)} %collective-permute-done.2), channel_id=1, source_target_pairs={{0,28},{4,0},{8,4},{12,8},{16,12},{20,16},{24,20},{28,24},{1,29},{... | collective-permute-start | bytes 24584 | tf_op jit(solution)/shard_map/ppermute | solution.py:18
  25.7 4.0 %collective-permute-start.5 = (bf16[8,512]{1,0:T(8,128)(2,1)S(1)}, bf16[8,512]{1,0:T(8,128)(2,1)S(1)}, u32[]{:S(2)}, u32[]{:S(2)}) collective-permute-start(bf16[8,512]{1,0:T(8,128)(2,1)S(1)} %collective-permute-done.3), channel_id=1, source_target_pairs={{0,4},{4,8},{8,12},{12,16},{16,20},{20,24},{24,28},{28,0},{1,5},{5... | collective-permute-start | bytes 24584 | tf_op jit(solution)/shard_map/ppermute | solution.py:15
  25.7 4.0 %collective-permute-start.6 = (bf16[8,512]{1,0:T(8,128)(2,1)S(1)}, bf16[8,512]{1,0:T(8,128)(2,1)S(1)}, u32[]{:S(2)}, u32[]{:S(2)}) collective-permute-start(bf16[8,512]{1,0:T(8,128)(2,1)S(1)} %collective-permute-done.4), channel_id=1, source_target_pairs={{0,28},{4,0},{8,4},{12,8},{16,12},{20,16},{24,20},{28,24},{1,29},{... | collective-permute-start | bytes 24584 | tf_op jit(solution)/shard_map/ppermute | solution.py:18
  29.6 4.0 %collective-permute-start.7 = (bf16[8,512]{1,0:T(8,128)(2,1)S(1)}, bf16[8,512]{1,0:T(8,128)(2,1)S(1)}, u32[]{:S(2)}, u32[]{:S(2)}) collective-permute-start(bf16[8,512]{1,0:T(8,128)(2,1)S(1)} %collective-permute-done.5), channel_id=1, source_target_pairs={{0,4},{4,8},{8,12},{12,16},{16,20},{20,24},{24,28},{28,0},{1,5},{5... | collective-permute-start | bytes 24584 | tf_op jit(solution)/shard_map/ppermute | solution.py:15
  33.7 2.0 %copy-start.1 = (s32[16,128,128]{2,1,0:T(8,128)S(1)}, s32[16,128,128]{2,1,0:T(8,128)}, u32[]{:S(2)}) copy-start(s32[16,128,128]{2,1,0:T(8,128)} %param.11) | copy-start | bytes 3145732
  38.3 1.2 copy-start.2
  38.3 1.3 copy-start.3
  43.7 79.5 %reduce-scatter.5.cloned.1.call-start = ((), (), s32[]{:S(2)}) async-start(), calls=%async_computation.4 | async-start | bytes 147456 | tf_op jit(solution)/shard_map/reduce_scatter | solution.py:72
  45.1 136.0 %all-reduce.2.cloned.1.call-start = ((), (), s32[]{:S(2)}) async-start(), calls=%async_computation.3 | async-start | bytes 1048576 | tf_op jit(solution)/shard_map/psum | solution.py:66
Sparse Core Ops, SparseCore 0:
  43.8 42.9 reduce-scatter.2
  90.3 32.7 reduce-scatter.4
  126.2 54.7 all-reduce.1
